TPU v7x, 32 devices: a whole 2x2x4 slice. The times are simulated.
32 devices in a mesh: groups: 2 (over y), ctx: 4 (over z), sub: 2 (over x), head: 2 (over core).
Axes of the slice: x: 2, y: 2, z: 4, core: 2. Of those that a mesh axis runs over, the one named last changes fastest.
Arguments:
- queries: bfloat16 [32, 10240, 128], P(('sub', 'head'), ('groups', 'ctx')), parts along dimension 1, may hold values from -6 to 6
- keys: bfloat16 [32, 10240, 128], P(('sub', 'head'), ('groups', 'ctx')), parts along dimension 1, may hold values from -6 to 6
- values: bfloat16 [32, 10240, 128], P(('sub', 'head'), ('groups', 'ctx')), parts along dimension 1, may hold values from -90 to 90
- out_grad: bfloat16 [32, 10240, 128], P(('sub', 'head'), ('groups', 'ctx')), parts along dimension 1, may hold values from -6 to 6
- norm_gain: float32 [32, 128], P(('sub', 'head')), may hold values from 0.25 to 1.75
- doc_ids: int32 [40], P(('groups', 'ctx')), parts along dimension 0, may hold values from 0 to 3, never falling along the last dimension, each value on 1 to 10 neighbouring positions
Outputs:
- grad_queries: bfloat16 [32, 10240, 128], P(('sub', 'head'), ('groups', 'ctx')), parts along dimension 1
- grad_keys: bfloat16 [32, 10240, 128], P(('sub', 'head'), ('groups', 'ctx')), parts along dimension 1
- grad_values: bfloat16 [32, 10240, 128], P(('sub', 'head'), ('groups', 'ctx')), parts along dimension 1
There are 2 independent parts, one for each index of `groups`. A program takes and returns all parts, laid end to end along the dimension named above; an argument that names none is the same for every part. Nothing has to cross between parts.
Inputs may be any that keep to these rules, and one draw needn't show every extreme that they name: `doc_ids`: never falls; each of its 4 values labels 1 to 10 consecutive blocks, one value exactly 10.
All inputs are finite; a program needn't handle non-finite values.
Results may differ from a plain program's by a relative error of at most 0.0058.
Values sent between devices are 32-bit elements; how exact they have to be, the bound alone decides.
No kernel may reach another device: no remote copies, remote signals or barrier semaphores. Data moves between devices by JAX's collectives and lax.ppermute only.
A program may use at most 128 MiB of HBM per device.

v0:
```python
import jax
import jax.numpy as jnp
from jax import lax
from jax.sharding import PartitionSpec as P


def carried_in(value, axis, combine, identity, reverse):
    peers, index = (lax.axis_size(axis), lax.axis_index(axis))
    everything = jax.tree.map(lambda part: lax.all_gather(part, axis), value)
    start = jax.tree.map(
        lambda part, zero: jnp.broadcast_to(jnp.asarray(zero, part.dtype), part.shape),
        value,
        identity,
    )

    def lap(k, before):
        at = peers - 1 - k if reverse else k
        reached = at > index if reverse else at < index
        new = combine(before, jax.tree.map(lambda part: part[at], everything))
        return jax.tree.map(lambda a, b: jnp.where(reached, a, b), new, before)

    return lax.fori_loop(0, peers, lap, start)


def carry_combine(earlier_part, later_part):
    joined = jnp.where(earlier_part[0] == later_part[0], 1.0, 0.0).astype(jnp.float32)
    return (later_part[0], later_part[1] + joined * earlier_part[1])


def on_device(queries, keys, values, out_grad, norm_gain, doc_ids):
    head_count, tok_count, head_width = queries.shape
    block_count = doc_ids.shape[0]
    block_len = tok_count // block_count
    block_shape = (head_count, block_count, block_len, head_width)
    highest_precision = lax.Precision.HIGHEST
    query_blocks = queries.reshape(block_shape)
    key_blocks = keys.reshape(block_shape)
    value_blocks = values.reshape(block_shape)
    row_ids = lax.broadcasted_iota(jnp.int32, (block_len, block_len), 0)
    col_ids = lax.broadcasted_iota(jnp.int32, (block_len, block_len), 1)
    causal = row_ids >= col_ids
    doc_values = doc_ids.astype(jnp.float32)
    block_pos = jnp.arange(block_count, dtype=jnp.int32)
    same_doc = doc_values[:, None] == doc_values[None, :]
    earlier_mask = (same_doc & (block_pos[None, :] < block_pos[:, None])).astype(jnp.float32)
    later_mask = (same_doc & (block_pos[None, :] > block_pos[:, None])).astype(jnp.float32)
    scores = jnp.einsum(
        "hnid,hnjd->hnij", query_blocks, key_blocks, preferred_element_type=jnp.float32
    )
    block_probs = jnp.where(causal, scores, 0.0).astype(jnp.bfloat16)
    intra_part = jnp.einsum(
        "hnij,hnjd->hnid", block_probs, value_blocks, preferred_element_type=jnp.float32
    )
    key_value_block = jnp.einsum(
        "hnid,hnie->hnde", key_blocks, value_blocks, preferred_element_type=jnp.float32
    )
    local_prefix = jnp.einsum(
        "bc,hcde->hbde", earlier_mask, key_value_block, precision=highest_precision
    )
    last_match = (doc_values == doc_values[-1]).astype(jnp.float32)
    device_kv = jnp.einsum("c,hcde->hde", last_match, key_value_block, precision=highest_precision)
    prior_doc, prior_state = carried_in(
        (doc_values[-1], device_kv),
        "ctx",
        carry_combine,
        (jnp.float32(-1.0), jnp.zeros_like(device_kv)),
        False,
    )
    prior_match = (doc_values == prior_doc).astype(jnp.float32)
    entering = prior_match[None, :, None, None] * prior_state[:, None, :, :]
    preceding_states = (local_prefix + entering).astype(jnp.bfloat16)
    cross_block_part = jnp.einsum(
        "hnid,hnde->hnie", query_blocks, preceding_states, preferred_element_type=jnp.float32
    )
    raw_attn = (intra_part + cross_block_part).reshape(head_count, tok_count, head_width)
    feature_count = head_count * head_width * lax.axis_size(("sub", "head"))
    scaled = norm_gain[:, None, :] * out_grad.astype(jnp.float32)
    square_total = lax.psum(jnp.sum(raw_attn * raw_attn, axis=(0, 2)), ("sub", "head"))
    root_mean = jnp.sqrt(square_total / feature_count + 1e-06)
    normed = raw_attn / root_mean[None, :, None]
    scaled_mean = lax.psum(jnp.sum(scaled * normed, axis=(0, 2)), ("sub", "head")) / feature_count
    d_attn = ((scaled - normed * scaled_mean[None, :, None]) / root_mean[None, :, None]).astype(
        jnp.bfloat16
    )
    output_grad_blocks = d_attn.reshape(block_shape)
    grad_scores = jnp.einsum(
        "hnid,hnjd->hnij", output_grad_blocks, value_blocks, preferred_element_type=jnp.float32
    )
    grad_probs = jnp.where(causal, grad_scores, 0.0).astype(jnp.bfloat16)
    query_gradient = jnp.einsum(
        "hnij,hnjd->hnid", grad_probs, key_blocks, preferred_element_type=jnp.float32
    )
    key_gradient = jnp.einsum(
        "hnij,hnid->hnjd", grad_probs, query_blocks, preferred_element_type=jnp.float32
    )
    value_gradient = jnp.einsum(
        "hnij,hnid->hnjd", block_probs, output_grad_blocks, preferred_element_type=jnp.float32
    )
    query_grad_block = jnp.einsum(
        "hnid,hnie->hnde", query_blocks, output_grad_blocks, preferred_element_type=jnp.float32
    )
    local_suffix = jnp.einsum(
        "bc,hcde->hbde", later_mask, query_grad_block, precision=highest_precision
    )
    first_match = (doc_values == doc_values[0]).astype(jnp.float32)
    device_qd = jnp.einsum(
        "c,hcde->hde", first_match, query_grad_block, precision=highest_precision
    )
    next_doc, next_state = carried_in(
        (doc_values[0], device_qd),
        "ctx",
        carry_combine,
        (jnp.float32(-1.0), jnp.zeros_like(device_qd)),
        True,
    )
    next_match = (doc_values == next_doc).astype(jnp.float32)
    leaving = next_match[None, :, None, None] * next_state[:, None, :, :]
    following_states = (local_suffix + leaving).astype(jnp.bfloat16)
    query_gradient = query_gradient + jnp.einsum(
        "hnie,hnde->hnid", output_grad_blocks, preceding_states, preferred_element_type=jnp.float32
    )
    key_gradient = key_gradient + jnp.einsum(
        "hnie,hnde->hnid", value_blocks, following_states, preferred_element_type=jnp.float32
    )
    value_gradient = value_gradient + jnp.einsum(
        "hnid,hnde->hnie", key_blocks, following_states, preferred_element_type=jnp.float32
    )
    out_shape = (head_count, tok_count, head_width)
    return (
        query_gradient.reshape(out_shape).astype(jnp.bfloat16),
        key_gradient.reshape(out_shape).astype(jnp.bfloat16),
        value_gradient.reshape(out_shape).astype(jnp.bfloat16),
    )


def solution(mesh):
    return jax.shard_map(
        on_device,
        mesh=mesh,
        in_specs=(
            P(("sub", "head"), ("groups", "ctx"), None),
            P(("sub", "head"), ("groups", "ctx"), None),
            P(("sub", "head"), ("groups", "ctx"), None),
            P(("sub", "head"), ("groups", "ctx"), None),
            P(("sub", "head"), None),
            P(("groups", "ctx")),
        ),
        out_specs=(
            P(("sub", "head"), ("groups", "ctx"), None),
            P(("sub", "head"), ("groups", "ctx"), None),
            P(("sub", "head"), ("groups", "ctx"), None),
        ),
        check_vma=False,
    )
```

profile of v0, /device:TPU:0, one launch (start us, length us, event | category | flops | bytes accessed | tf_op | source)
XLA Modules:
  0.0 199.0 jit_solution(3285715845271670284)
XLA Ops:
  7.2 0.0 copy-start
  7.2 0.0 all-gather.5.cloned.1.call-start
  7.2 0.8 convert_element_type.51
  8.0 1.2 dynamic-slice
  9.3 3.4 %fusion.30 = f32[8,5,128,128]{3,2,1,0:T(8,128)S(1)} fusion(bf16[8,5,256,128]{3,2,1,0:T(8,128)(2,1)} %bitcast.118, bf16[8,5,256,128]{3,2,1,0:T(8,128)(2,1)} %bitcast.122), kind=kOutput, calls=%fused_computation.55 | convolution fusion | flops 335544320 | bytes 7864320 | tf_op jit(solution)/shard_map/hnid,hnie->hnde/dot_general | solution.py:54
  12.7 0.0 copy-start.1
  12.7 1.4 fusion.28
  14.1 0.1 copy-done.1
  14.2 4.8 %fusion.4 = f32[1,8,128,128]{3,0,2,1:T(1,128)} fusion(f32[8,5,128,128]{3,2,1,0:T(8,128)S(1)} %fusion.30, f32[]{:T(128)} %bitcast.8, s32[5]{0:T(128)S(1)} %copy-done.15), kind=kOutput, calls=%fused_computation.17 | convolution fusion | flops 7864330 | bytes 3145752 | tf_op jit(solution)/shard_map/c,hcde->hde/dot_general | solution.py:61
  19.0 0.0 all-gather.5.cloned.1.call-update
  19.0 0.0 all-gather.7.cloned.1.call-start
  19.1 0.7 slice_dynamic-update-slice_fusion
  19.9 13.7 %all-reduce.2 = (f32[4]{0:T(128)S(1)}, f32[4]{0:T(128)S(1)}) all-reduce(f32[4]{0:T(128)S(1)} %get-tuple-element.341, f32[4]{0:T(128)S(1)} %slice_dynamic-update-slice_fusion), channel_id=1, replica_groups=mesh['groups'=2,'ctx'=4,'sub'=2,'head'=2] {'ctx'}, use_global_device_ids=true, to_apply=%add | all-reduce | flops 8 | bytes 64
  33.6 0.0 copy-start.6
  33.6 7.4 %fusion.6 = f32[8,128,128,5]{2,3,1,0:T(8,128)} fusion(f32[8,5,128,128]{3,2,1,0:T(8,128)} %copy-done.1, f32[5]{0:T(128)S(1)} %convert_element_type.51), kind=kOutput, calls=%fused_computation.19 | convolution fusion | flops 39321676 | bytes 5242900 | tf_op jit(solution)/shard_map/bc,hcde->hbde/dot_general | solution.py:57
  41.0 1.5 select_convert_fusion.1
  42.5 2.3 %copy-done.4 = bf16[8,5,256,256]{3,2,1,0:T(8,128)(2,1)} copy-done((bf16[8,5,256,256]{3,2,1,0:T(8,128)(2,1)}, bf16[8,5,256,256]{3,2,1,0:T(8,128)(2,1)S(1)}, u32[]{:S(2)}) %copy-start.4) | copy-done | bytes 5242904
  44.8 3.9 %fusion.29 = f32[8,5,256,128]{3,2,1,0:T(8,128)} fusion(bf16[8,5,256,256]{3,2,1,0:T(8,128)(2,1)S(1)} %select_convert_fusion.1, bf16[8,5,256,128]{3,2,1,0:T(8,128)(2,1)S(1)} %bitcast.123), kind=kOutput, calls=%fused_computation.54 | convolution fusion | flops 671088640 | bytes 13107200 | tf_op jit(solution)/shard_map/hnij,hnjd->hnid/dot_general | solution.py:51
  48.7 19.1 %all-gather.5.cloned.1.call-done = f32[32,128,128]{2,1,0:T(8,128)} async-done(((f32[8,128,128]{2,1,0:T(8,128)}), f32[32,128,128]{2,1,0:T(8,128)}) %all-gather.5.cloned.1.call-update) | async-done | bytes 2097168 | tf_op jit(solution)/shard_map/all_gather | solution.py:9
  67.8 13.5 %while.34 = (s32[]{:T(128)}, f32[]{:T(128)}, f32[8,128,128]{2,1,0:T(8,128)S(1)}, s32[]{:T(128)}, f32[4]{0:T(128)S(1)}, /*index=5*/f32[4,8,128,128]{3,2,1,0:T(8,128)}, s32[]{:T(128)}, f32[]{:T(128)}, f32[]{:T(128)}, s32[]{:T(128)}) while((s32[]{:T(128)}, f32[]{:T(128)}, f32[8,128,128]{2,1,0:T(8,128)S(1)}, s32[]{:T(128)}, ...), condition=%wide.region_1.2_spmd.clone, body=%wide.region_0.1_spmd.clone.sunk | while | flops 524295 | bytes 1573048 | solution.py:22
  67.8 0.6 dynamic_slice.45
  69.7 1.5 fusion.62
  71.2 0.6 dynamic_slice.45
  73.1 1.5 fusion.62
  74.6 0.6 dynamic_slice.45
  76.5 1.5 fusion.62
  78.0 0.6 dynamic_slice.45
  79.9 1.5 fusion.62
  81.4 3.0 %fusion.9 = bf16[8,5,128,128]{3,2,1,0:T(8,128)(2,1)S(1)} fusion(f32[8,128,128,5]{2,3,1,0:T(8,128)} %fusion.6, f32[8,128,128]{2,1,0:T(8,128)S(1)} %get-tuple-element.269, f32[5]{0:T(128)S(1)} %compare_convert_fusion.1), kind=kLoop, calls=%fused_computation.24 | loop fusion | flops 1966080 | bytes 4456468 | tf_op jit(solution)/shard_map/convert_element_type | solution.py:71
  84.4 0.8 copy-done.5
  85.2 3.2 %multiply_reduce_fusion.1 = (f32[5,256]{1,0:T(8,128)S(1)}, f32[8,5,256,128]{3,2,1,0:T(8,128)}) fusion(f32[8,5,256,128]{3,2,1,0:T(8,128)S(1)} %copy-done.5, bf16[8,5,256,128]{3,2,1,0:T(8,128)(2,1)S(1)} %bitcast.109, bf16[8,5,128,128]{3,2,1,0:T(8,128)(2,1)S(1)} %fusion.9), kind=kOutput, calls=%fused_computation.15 | convolution fusion | flops 339475200 | bytes 14423040 | tf_op jit(solution)/shard_map/hnid,hnde->hnie/dot_general | solution.py:72
  88.4 7.0 %psum.14 = f32[1280]{0:T(1024)S(1)} all-reduce(f32[1280]{0:T(1024)S(1)} %reduce_sum.21), channel_id=1, replica_groups=mesh['groups'=2,'ctx'=4,'sub'=2,'head'=2] {'sub','head'}, use_global_device_ids=true, to_apply=%region_3.4 | all-reduce | flops 1280 | bytes 10240 | tf_op jit(solution)/shard_map/psum | solution.py:78
  95.4 4.3 %multiply_reduce_fusion = f32[1280]{0:T(1024)S(1)} fusion(bf16[8,1280,128]{2,1,0:T(8,128)(2,1)} %param.13, f32[8,128]{1,0:T(8,128)S(1)} %copy-done.14, f32[1280]{0:T(1024)S(1)} %add_sqrt_fusion, f32[8,5,256,128]{3,2,1,0:T(8,128)} %get-tuple-element.344), kind=kLoop, calls=%fused_computation.14 | loop fusion | flops 6552320 | bytes 7878656 | tf_op jit(solution)/shard_map/reduce_sum | solution.py:81
  99.7 6.0 %psum.15 = f32[1280]{0:T(1024)S(1)} all-reduce(f32[1280]{0:T(1024)S(1)} %multiply_reduce_fusion), channel_id=1, replica_groups=mesh['groups'=2,'ctx'=4,'sub'=2,'head'=2] {'sub','head'}, use_global_device_ids=true, to_apply=%region_5.6 | all-reduce | flops 1280 | bytes 10240 | tf_op jit(solution)/shard_map/psum | solution.py:81
  105.7 4.1 %divide_convert_fusion = bf16[8,1280,128]{2,1,0:T(8,128)(2,1)S(1)} fusion(bf16[8,1280,128]{2,1,0:T(8,128)(2,1)} %param.13, f32[1280]{0:T(1024)S(1)} %broadcast_multiply_fusion, f32[1280]{0:T(1024)S(1)} %add_sqrt_fusion, f32[8,128]{1,0:T(8,128)S(1)} %copy-done.14, f32[8,5,256,128]{3,2,1,0:T(8,128)} %get-tuple-element.344), kind=kLoop, calls=%fused_computation.13 | loop fusion | flops 9175040 | bytes 10500096 | tf_op jit(solution)/shard_map/convert_element_type | solution.py:82
  109.9 0.0 copy-start.2
  109.9 1.5 copy-done.2
  111.4 2.4 %convolution_bitcast_fusion = f32[8,5,128,128]{2,3,1,0:T(8,128)} fusion(bf16[8,5,256,128]{3,2,1,0:T(8,128)(2,1)S(1)} %bitcast.112, bf16[8,5,256,128]{3,2,1,0:T(8,128)(2,1)S(1)} %bitcast.111), kind=kOutput, calls=%fused_computation.25 | convolution fusion | flops 335544320 | bytes 7864320 | tf_op jit(solution)/shard_map/hnid,hnie->hnde/dot_general | solution.py:99
  113.7 4.8 %copy.42 = f32[8,5,128,128]{3,1,2,0:T(8,128)} copy(f32[8,5,128,128]{2,3,1,0:T(8,128)} %convolution_bitcast_fusion) | data formatting | bytes 5242880 | tf_op jit(solution)/shard_map/hnid,hnie->hnde/dot_general | solution.py:99
  118.5 5.7 %fusion.19 = f32[1,8,128,128]{3,0,2,1:T(1,128)} fusion(f32[8,5,128,128]{3,1,2,0:T(8,128)} %copy.42, f32[]{:T(128)} %bitcast.23, s32[5]{0:T(128)S(1)} %copy-done.15), kind=kOutput, calls=%fused_computation.40 | convolution fusion | flops 7864330 | bytes 3145752 | tf_op jit(solution)/shard_map/c,hcde->hde/dot_general | solution.py:106
  124.2 0.0 all-gather.7.cloned.1.call-update
  124.2 0.0 copy-start.3
  124.3 6.6 %fusion.13 = f32[8,128,128,5]{2,3,1,0:T(8,128)} fusion(f32[8,5,128,128]{3,1,2,0:T(8,128)} %copy.42, f32[5]{0:T(128)S(1)} %convert_element_type.51), kind=kOutput, calls=%fused_computation.35 | convolution fusion | flops 39321676 | bytes 5242900 | tf_op jit(solution)/shard_map/bc,hcde->hbde/dot_general | solution.py:102
  130.8 1.5 select_convert_fusion
  132.4 0.2 copy-done.7
  132.6 1.5 fusion.31
  134.1 0.0 copy-done.13
  134.1 2.4 %add_convert_fusion = bf16[8,5,256,128]{3,2,1,0:T(8,128)(2,1)} fusion(f32[8,5,256,128]{3,2,1,0:T(8,128)S(1)} %fusion.31, bf16[8,5,256,128]{3,2,1,0:T(8,128)(2,1)S(1)} %bitcast.114, bf16[8,5,128,128]{3,2,1,0:T(8,128)(2,1)S(1)} %copy-done.13), kind=kOutput, calls=%fused_computation.12 | convolution fusion | flops 338165760 | bytes 11796480 | tf_op jit(solution)/shard_map/hnie,hnde->hnid/dot_general | solution.py:119
  136.6 3.9 %fusion.33 = f32[8,5,256,128]{3,2,1,0:T(8,128)} fusion(bf16[8,5,256,256]{3,2,1,0:T(8,128)(2,1)S(1)} %bitcast.117, bf16[8,5,256,128]{3,2,1,0:T(8,128)(2,1)S(1)} %bitcast.115), kind=kOutput, calls=%fused_computation.58 | convolution fusion | flops 671088640 | bytes 13107200 | tf_op jit(solution)/shard_map/hnij,hnid->hnjd/dot_general | solution.py:96
  140.5 3.9 %fusion.32 = f32[8,5,256,128]{3,2,1,0:T(8,128)} fusion(bf16[8,5,256,256]{3,2,1,0:T(8,128)(2,1)S(1)} %select_convert_fusion, bf16[8,5,256,128]{3,2,1,0:T(8,128)(2,1)S(1)} %bitcast.110), kind=kOutput, calls=%fused_computation.57 | convolution fusion | flops 671088640 | bytes 13107200 | tf_op jit(solution)/shard_map/hnij,hnid->hnjd/dot_general | solution.py:93
  144.4 23.7 %all-gather.7.cloned.1.call-done = f32[32,128,128]{2,1,0:T(8,128)} async-done(((f32[8,128,128]{2,1,0:T(8,128)}), f32[32,128,128]{2,1,0:T(8,128)}) %all-gather.7.cloned.1.call-update) | async-done | bytes 2097168 | tf_op jit(solution)/shard_map/all_gather | solution.py:9
  168.1 13.6 %while.35 = (s32[]{:T(128)}, f32[]{:T(128)}, f32[8,128,128]{2,1,0:T(8,128)S(1)}, s32[]{:T(128)}, f32[4]{0:T(128)S(1)}, /*index=5*/f32[4,8,128,128]{3,2,1,0:T(8,1...) while((s32[]{:T(128)}, f32[]{:T(128)}, ...), condition=%wide.region_7.8_spmd.clone, body=%wide.region_6.7_spmd.clone.sunk | while | flops 524299 | bytes 1573110 | solution.py:22
  168.1 0.6 dynamic_slice.47
  170.0 1.5 fusion.63
  171.5 0.6 dynamic_slice.47
  173.4 1.5 fusion.63
  174.9 0.6 dynamic_slice.47
  176.8 1.5 fusion.63
  178.3 0.6 dynamic_slice.47
  180.2 1.5 fusion.63
  181.7 3.0 %fusion.8 = bf16[8,5,128,128]{3,2,1,0:T(8,128)(2,1)S(1)} fusion(f32[8,128,128,5]{2,3,1,0:T(8,128)} %fusion.13, f32[8,128,128]{2,1,0:T(8,128)S(1)} %get-tuple-element.271, f32[5]{0:T(128)S(1)} %compare_convert_fusion), kind=kLoop, calls=%fused_computation.22 | loop fusion | flops 1966080 | bytes 4456468 | tf_op jit(solution)/shard_map/convert_element_type | solution.py:118
  184.7 0.0 copy-done.8
  184.7 5.1 %fusion.2 = bf16[8,5,256,128]{3,2,1,0:T(8,128)(2,1)} fusion(f32[8,5,256,128]{3,2,1,0:T(8,128)} %fusion.33, bf16[8,5,256,128]{3,2,1,0:T(8,128)(2,1)S(1)} %bitcast.121, bf16[8,5,128,128]{3,2,1,0:T(8,128)(2,1)S(1)} %fusion.8), kind=kOutput, calls=%fused_computation.7 | convolution fusion | flops 338165760 | bytes 11796480 | tf_op jit(solution)/shard_map/hnid,hnde->hnie/dot_general | solution.py:125
  189.9 2.3 %fusion.3 = bf16[8,5,256,128]{3,2,1,0:T(8,128)(2,1)} fusion(f32[8,5,256,128]{3,2,1,0:T(8,128)S(1)} %bitcast.127, bf16[8,5,128,128]{3,2,1,0:T(8,128)(2,1)S(1)} %fusion.8, bf16[8,5,256,128]{3,2,1,0:T(8,128)(2,1)S(1)} %bitcast.125), kind=kOutput, calls=%fused_computation.9 | convolution fusion | flops 338165760 | bytes 11796480 | tf_op jit(solution)/shard_map/hnie,hnde->hnid/dot_general | solution.py:122
  (40 shorter events, 0.1 us)
Async XLA Ops:
  7.2 33.8 %copy-start = (bf16[8,1280,128]{2,1,0:T(8,128)(2,1)S(1)}, bf16[8,1280,128]{2,1,0:T(8,128)(2,1)}, u32[]{:S(2)}) copy-start(bf16[8,1280,128]{2,1,0:T(8,128)(2,1)} %param.10) | copy-start | bytes 7864324
  7.2 60.7 %all-gather.5.cloned.1.call-start = ((), (), s32[]{:S(2)}) async-start(), calls=%async_computation | async-start | bytes 2621440 | tf_op jit(solution)/shard_map/all_gather | solution.py:9
  9.3 4.9 %copy-start.15 = (s32[5]{0:T(128)S(1)}, s32[5]{0:T(128)}, u32[]{:S(2)}) copy-start(s32[5]{0:T(128)} %param.15) | copy-start | bytes 64
  12.7 1.5 copy-start.1
  19.0 149.1 %all-gather.7.cloned.1.call-start = ((), (), s32[]{:S(2)}) async-start(), calls=%async_computation.1 | async-start | bytes 2621440 | tf_op jit(solution)/shard_map/all_gather | solution.py:9
  33.6 7.4 %copy-start.6 = (bf16[8,1280,128]{2,1,0:T(8,128)(2,1)S(1)}, bf16[8,1280,128]{2,1,0:T(8,128)(2,1)}, u32[]{:S(2)}) copy-start(bf16[8,1280,128]{2,1,0:T(8,128)(2,1)} %param.11) | copy-start | bytes 7864324
  41.0 3.9 %copy-start.9 = (bf16[8,1280,128]{2,1,0:T(8,128)(2,1)S(1)}, bf16[8,1280,128]{2,1,0:T(8,128)(2,1)}, u32[]{:S(2)}) copy-start(bf16[8,1280,128]{2,1,0:T(8,128)(2,1)} %param.12) | copy-start | bytes 7864324
  42.5 2.3 %copy-start.4 = (bf16[8,5,256,256]{3,2,1,0:T(8,128)(2,1)}, bf16[8,5,256,256]{3,2,1,0:T(8,128)(2,1)S(1)}, u32[]{:S(2)}) copy-start(bf16[8,5,256,256]{3,2,1,0:T(8,128)(2,1)S(1)} %select_convert_fusion.1) | copy-start | bytes 15728644
  81.4 3.7 %copy-start.5 = (f32[8,5,256,128]{3,2,1,0:T(8,128)S(1)}, f32[8,5,256,128]{3,2,1,0:T(8,128)}, u32[]{:S(2)}) copy-start(f32[8,5,256,128]{3,2,1,0:T(8,128)} %fusion.29) | copy-start | bytes 15728644
  85.2 3.2 %copy-start.12 = (bf16[8,5,128,128]{3,2,1,0:T(8,128)(2,1)}, bf16[8,5,128,128]{3,2,1,0:T(8,128)(2,1)S(1)}, u32[]{:S(2)}) copy-start(bf16[8,5,128,128]{3,2,1,0:T(8,128)(2,1)S(1)} %fusion.9) | copy-start | bytes 3932164
  85.2 10.3 %copy-start.14 = (f32[8,128]{1,0:T(8,128)S(1)}, f32[8,128]{1,0:T(8,128)}, u32[]{:S(2)}) copy-start(f32[8,128]{1,0:T(8,128)} %param.14) | copy-start | bytes 12292
  109.9 1.5 copy-start.2
  124.2 6.6 %copy-start.3 = (bf16[8,1280,128]{2,1,0:T(8,128)(2,1)S(1)}, bf16[8,1280,128]{2,1,0:T(8,128)(2,1)}, u32[]{:S(2)}) copy-start(bf16[8,1280,128]{2,1,0:T(8,128)(2,1)} %copy-done.2) | copy-start | bytes 7864324
  124.2 6.6 %copy-start.10 = (bf16[8,1280,128]{2,1,0:T(8,128)(2,1)S(1)}, bf16[8,1280,128]{2,1,0:T(8,128)(2,1)}, u32[]{:S(2)}) copy-start(bf16[8,1280,128]{2,1,0:T(8,128)(2,1)} %param.12) | copy-start | bytes 7864324
  130.8 1.7 copy-start.7
  130.8 5.7 %slice-start = ((s8[5242880]{0:T(1024)(128)(4,1)}), s8[4194304]{0:T(1024)(128)(4,1)S(1)}, s32[]{:S(2)}) async-start(s8[5242880]{0:T(1024)(128)(4,1)} %bitcast.116), calls=%async_computation.2 | async-start | bytes 8388608
  132.6 1.6 copy-start.13
  132.6 4.0 %slice-start.1 = ((s8[5242880]{0:T(1024)(128)(4,1)}), s8[1048576]{0:T(1024)(128)(4,1)S(1)}, s32[]{:S(2)}) async-start(s8[5242880]{0:T(1024)(128)(4,1)} %bitcast.116), calls=%async_computation.3 | async-start | bytes 2097152
  181.7 3.0 %copy-start.8 = (bf16[8,1280,128]{2,1,0:T(8,128)(2,1)S(1)}, bf16[8,1280,128]{2,1,0:T(8,128)(2,1)}, u32[]{:S(2)}) copy-start(bf16[8,1280,128]{2,1,0:T(8,128)(2,1)} %param.11) | copy-start | bytes 7864324
  181.7 8.1 %slice-start.2 = ((s8[5242880]{0:T(1024)(128)(4,1)}), s8[4194304]{0:T(1024)(128)(4,1)S(1)}, s32[]{:S(2)}) async-start(s8[5242880]{0:T(1024)(128)(4,1)} %bitcast.126), calls=%async_computation.4 | async-start | bytes 8388608
  184.7 5.1 %copy-start.11 = (bf16[8,1280,128]{2,1,0:T(8,128)(2,1)S(1)}, bf16[8,1280,128]{2,1,0:T(8,128)(2,1)}, u32[]{:S(2)}) copy-start(bf16[8,1280,128]{2,1,0:T(8,128)(2,1)} %param.12) | copy-start | bytes 7864324
  184.7 5.1 %slice-start.3 = ((s8[5242880]{0:T(1024)(128)(4,1)}), s8[1048576]{0:T(1024)(128)(4,1)S(1)}, s32[]{:S(2)}) async-start(s8[5242880]{0:T(1024)(128)(4,1)} %bitcast.126), calls=%async_computation.5 | async-start | bytes 2097152
Sparse Core Ops, SparseCore 0:
  19.2 48.6 all-gather.4
  124.3 43.7 all-gather.6
where the time goes:
time: 200 us; the launch traced here: 199 us
  matrix products  59.6 us (30%)
  waiting for transfers between devices  42.9 us (21%)
  other arithmetic  27 us (14%)
  blocking collectives  26.7 us (13%)
  local copies, waits for them, and re-layouts  17.8 us (9%)
  between operations  14.3 us (7%)
  loops' own time  10.6 us (5%)
    all_gather x2, waiting for transfers between devices, carried_in(): everything = jax.tree.map(lambda part: lax.all_gather(part, axis), value)  42.9 us
    unnamed x1, blocking collectives  13.7 us
    select_n x8, other arithmetic, lap(): return jax.tree.map(lambda a, b: jnp.where(reached, a, b), new, before)  11.8 us
    another operation x2, loops' own time, carried_in(): return lax.fori_loop(0, peers, lap, start)  10.6 us
    dot_general x1, matrix products, on_device(): jnp.einsum('bc,hcde->hbde', earlier_mask, key_value_block, precision=high...  7.38 us
    psum x1, blocking collectives, on_device(): lax.psum(jnp.sum(raw_attn * raw_attn, axis=(0, 2)), ('sub', 'head'))  7 us
    unnamed x44, local copies, waits for them, and re-layouts  6.97 us
    dot_general x1, matrix products, on_device(): jnp.einsum('bc,hcde->hbde', later_mask, query_grad_block, precision=highe...  6.56 us
  transfers between devices with their start and end apart: 2, of which 2 were waited for; matrix products, arithmetic and copies ran while one was open for 17% of the time, Pallas kernels for 0%

commit v1 on v0

--- a/solution.py
+++ b/solution.py
@@ -75,7 +75,8 @@
     raw_attn = (intra_part + cross_block_part).reshape(head_count, tok_count, head_width)
     feature_count = head_count * head_width * lax.axis_size(("sub", "head"))
     scaled = norm_gain[:, None, :] * out_grad.astype(jnp.float32)
-    square_total = lax.psum(jnp.sum(raw_attn * raw_attn, axis=(0, 2)), ("sub", "head"))
+    raw = jnp.sum(raw_attn * raw_attn, axis=(0, 2))
+    square_total = jnp.sum(lax.all_gather(raw, ("sub", "head")), 0)
     root_mean = jnp.sqrt(square_total / feature_count + 1e-06)
     normed = raw_attn / root_mean[None, :, None]
     scaled_mean = lax.psum(jnp.sum(scaled * normed, axis=(0, 2)), ("sub", "head")) / feature_count

time: 200 us -> 199 us (level)
    psum x1 -> x0, blocking collectives: 7 us -> none  [on_device(): lax.psum(jnp.sum(raw_attn * raw_attn, axis=(0, 2)), ('sub', 'head'))]
    all_gather x0 -> x1, blocking collectives: none -> 5.19 us  [on_device(): square_total = jnp.sum(lax.all_gather(raw, ('sub', 'head')), 0)]
    unnamed x44 -> x45, local copies, waits for them, and re-layouts: 6.97 us -> 6.98 us
where the time goes in v1:
time: 199 us; the launch traced here: 198 us
  matrix products  59.6 us (30%)
  waiting for transfers between devices  42.9 us (22%)
  other arithmetic  27.1 us (14%)
  blocking collectives  26 us (13%)
  local copies, waits for them, and re-layouts  17.8 us (9%)
  between operations  14.3 us (7%)
  loops' own time  10.6 us (5%)
    all_gather x2, waiting for transfers between devices, carried_in(): everything = jax.tree.map(lambda part: lax.all_gather(part, axis), value)  42.8 us
    unnamed x1, blocking collectives  13.7 us
    select_n x8, other arithmetic, lap(): return jax.tree.map(lambda a, b: jnp.where(reached, a, b), new, before)  11.8 us
    another operation x2, loops' own time, carried_in(): return lax.fori_loop(0, peers, lap, start)  10.6 us
    dot_general x1, matrix products, on_device(): jnp.einsum('bc,hcde->hbde', earlier_mask, key_value_block, precision=high...  7.38 us
    psum x1, blocking collectives, on_device(): lax.psum(jnp.sum(scaled * normed, axis=(0, 2)), ('sub', 'head'))  7.14 us
    unnamed x45, local copies, waits for them, and re-layouts  6.98 us
    dot_general x1, matrix products, on_device(): jnp.einsum('bc,hcde->hbde', later_mask, query_grad_block, precision=highe...  6.56 us
  transfers between devices with their start and end apart: 2, of which 2 were waited for; matrix products, arithmetic and copies ran while one was open for 17% of the time, Pallas kernels for 0%

profile of v1, /device:TPU:0, one launch (start us, length us, event | category | flops | bytes accessed | tf_op | source)
XLA Modules:
  0.0 198.4 jit_solution(11288232074622068356)
XLA Ops:
  7.2 0.0 copy-start
  7.2 0.0 all-gather.6.cloned.1.call-start
  7.2 0.8 convert_element_type.51
  8.0 1.2 dynamic-slice
  9.3 3.4 %fusion.30 = f32[8,5,128,128]{3,2,1,0:T(8,128)S(1)} fusion(bf16[8,5,256,128]{3,2,1,0:T(8,128)(2,1)} %bitcast.118, bf16[8,5,256,128]{3,2,1,0:T(8,128)(2,1)} %bitcast.122), kind=kOutput, calls=%fused_computation.55 | convolution fusion | flops 335544320 | bytes 7864320 | tf_op jit(solution)/shard_map/hnid,hnie->hnde/dot_general | solution.py:54
  12.7 0.0 copy-start.1
  12.7 1.4 fusion.28
  14.1 0.1 copy-done.1
  14.2 4.8 %fusion.4 = f32[1,8,128,128]{3,0,2,1:T(1,128)} fusion(f32[8,5,128,128]{3,2,1,0:T(8,128)S(1)} %fusion.30, f32[]{:T(128)} %bitcast.8, s32[5]{0:T(128)S(1)} %copy-done.15), kind=kOutput, calls=%fused_computation.17 | convolution fusion | flops 7864330 | bytes 3145752 | tf_op jit(solution)/shard_map/c,hcde->hde/dot_general | solution.py:61
  19.0 0.0 all-gather.6.cloned.1.call-update
  19.0 0.0 all-gather.8.cloned.1.call-start
  19.1 0.7 slice_dynamic-update-slice_fusion
  19.9 13.7 %all-reduce.2 = (f32[4]{0:T(128)S(1)}, f32[4]{0:T(128)S(1)}) all-reduce(f32[4]{0:T(128)S(1)} %get-tuple-element.341, f32[4]{0:T(128)S(1)} %slice_dynamic-update-slice_fusion), channel_id=1, replica_groups=mesh['groups'=2,'ctx'=4,'sub'=2,'head'=2] {'ctx'}, use_global_device_ids=true, to_apply=%add | all-reduce | flops 8 | bytes 64
  33.6 0.0 copy-start.6
  33.6 7.4 %fusion.6 = f32[8,128,128,5]{2,3,1,0:T(8,128)} fusion(f32[8,5,128,128]{3,2,1,0:T(8,128)} %copy-done.1, f32[5]{0:T(128)S(1)} %convert_element_type.51), kind=kOutput, calls=%fused_computation.19 | convolution fusion | flops 39321676 | bytes 5242900 | tf_op jit(solution)/shard_map/bc,hcde->hbde/dot_general | solution.py:57
  41.0 1.5 select_convert_fusion.1
  42.5 2.3 %copy-done.4 = bf16[8,5,256,256]{3,2,1,0:T(8,128)(2,1)} copy-done((bf16[8,5,256,256]{3,2,1,0:T(8,128)(2,1)}, bf16[8,5,256,256]{3,2,1,0:T(8,128)(2,1)S(1)}, u32[]{:S(2)}) %copy-start.4) | copy-done | bytes 5242904
  44.8 3.9 %fusion.29 = f32[8,5,256,128]{3,2,1,0:T(8,128)} fusion(bf16[8,5,256,256]{3,2,1,0:T(8,128)(2,1)S(1)} %select_convert_fusion.1, bf16[8,5,256,128]{3,2,1,0:T(8,128)(2,1)S(1)} %bitcast.123), kind=kOutput, calls=%fused_computation.54 | convolution fusion | flops 671088640 | bytes 13107200 | tf_op jit(solution)/shard_map/hnij,hnjd->hnid/dot_general | solution.py:51
  48.7 19.1 %all-gather.6.cloned.1.call-done = f32[32,128,128]{2,1,0:T(8,128)} async-done(((f32[8,128,128]{2,1,0:T(8,128)}), f32[32,128,128]{2,1,0:T(8,128)}) %all-gather.6.cloned.1.call-update) | async-done | bytes 2097168 | tf_op jit(solution)/shard_map/all_gather | solution.py:9
  67.8 13.5 %while.34 = (s32[]{:T(128)}, f32[]{:T(128)}, f32[8,128,128]{2,1,0:T(8,128)S(1)}, s32[]{:T(128)}, f32[4]{0:T(128)S(1)}, /*index=5*/f32[4,8,128,128]{3,2,1,0:T(8,128)}, s32[]{:T(128)}, f32[]{:T(128)}, f32[]{:T(128)}, s32[]{:T(128)}) while((s32[]{:T(128)}, f32[]{:T(128)}, f32[8,128,128]{2,1,0:T(8,128)S(1)}, s32[]{:T(128)}, ...), condition=%wide.region_1.2_spmd.clone, body=%wide.region_0.1_spmd.clone.sunk | while | flops 524295 | bytes 1573048 | solution.py:22
  67.8 0.6 dynamic_slice.45
  69.7 1.5 fusion.62
  71.2 0.6 dynamic_slice.45
  73.1 1.5 fusion.62
  74.6 0.6 dynamic_slice.45
  76.5 1.5 fusion.62
  78.0 0.6 dynamic_slice.45
  79.9 1.5 fusion.62
  81.4 3.0 %fusion.9 = bf16[8,5,128,128]{3,2,1,0:T(8,128)(2,1)S(1)} fusion(f32[8,128,128,5]{2,3,1,0:T(8,128)} %fusion.6, f32[8,128,128]{2,1,0:T(8,128)S(1)} %get-tuple-element.269, f32[5]{0:T(128)S(1)} %compare_convert_fusion.1), kind=kLoop, calls=%fused_computation.24 | loop fusion | flops 1966080 | bytes 4456468 | tf_op jit(solution)/shard_map/convert_element_type | solution.py:71
  84.4 0.8 copy-done.5
  85.2 3.2 %multiply_reduce_fusion.1 = (f32[5,256]{1,0:T(8,128)S(1)}, f32[8,5,256,128]{3,2,1,0:T(8,128)}) fusion(f32[8,5,256,128]{3,2,1,0:T(8,128)S(1)} %copy-done.5, bf16[8,5,256,128]{3,2,1,0:T(8,128)(2,1)S(1)} %bitcast.109, bf16[8,5,128,128]{3,2,1,0:T(8,128)(2,1)S(1)} %fusion.9), kind=kOutput, calls=%fused_computation.15 | convolution fusion | flops 339475200 | bytes 14423040 | tf_op jit(solution)/shard_map/hnid,hnde->hnie/dot_general | solution.py:72
  88.4 5.2 %all-gather.2 = f32[4,1,1280]{2,1,0:T(1,128)S(1)} all-gather(f32[1,1,1280]{2,1,0:T(1,128)S(1)} %reshape.55), channel_id=1, replica_groups=mesh['groups'=2,'ctx'=4,'sub'=2,'head'=2] {'sub','head'}, dimensions={0}, use_global_device_ids=true | all-gather | bytes 25600 | tf_op jit(solution)/shard_map/all_gather | solution.py:79
  93.7 4.3 %multiply_reduce_fusion = f32[1280]{0:T(1024)S(1)} fusion(bf16[8,1280,128]{2,1,0:T(8,128)(2,1)} %param.13, f32[8,128]{1,0:T(8,128)S(1)} %copy-done.14, f32[1280]{0:T(1024)S(1)} %add_sqrt_fusion, f32[8,5,256,128]{3,2,1,0:T(8,128)} %get-tuple-element.344), kind=kLoop, calls=%fused_computation.14 | loop fusion | flops 6552320 | bytes 7878656 | tf_op jit(solution)/shard_map/reduce_sum | solution.py:82
  97.9 7.1 %psum.7 = f32[1280]{0:T(1024)S(1)} all-reduce(f32[1280]{0:T(1024)S(1)} %multiply_reduce_fusion), channel_id=1, replica_groups=mesh['groups'=2,'ctx'=4,'sub'=2,'head'=2] {'sub','head'}, use_global_device_ids=true, to_apply=%region_5.6 | all-reduce | flops 1280 | bytes 10240 | tf_op jit(solution)/shard_map/psum | solution.py:82
  105.1 4.1 %divide_convert_fusion = bf16[8,1280,128]{2,1,0:T(8,128)(2,1)S(1)} fusion(bf16[8,1280,128]{2,1,0:T(8,128)(2,1)} %param.13, f32[1280]{0:T(1024)S(1)} %broadcast_multiply_fusion, f32[1280]{0:T(1024)S(1)} %add_sqrt_fusion, f32[8,128]{1,0:T(8,128)S(1)} %copy-done.14, f32[8,5,256,128]{3,2,1,0:T(8,128)} %get-tuple-element.344), kind=kLoop, calls=%fused_computation.13 | loop fusion | flops 9175040 | bytes 10500096 | tf_op jit(solution)/shard_map/convert_element_type | solution.py:83
  109.2 1.5 copy-done.2
  110.7 2.4 %convolution_bitcast_fusion = f32[8,5,128,128]{2,3,1,0:T(8,128)} fusion(bf16[8,5,256,128]{3,2,1,0:T(8,128)(2,1)S(1)} %bitcast.112, bf16[8,5,256,128]{3,2,1,0:T(8,128)(2,1)S(1)} %bitcast.111), kind=kOutput, calls=%fused_computation.25 | convolution fusion | flops 335544320 | bytes 7864320 | tf_op jit(solution)/shard_map/hnid,hnie->hnde/dot_general | solution.py:100
  113.1 4.8 %copy.42 = f32[8,5,128,128]{3,1,2,0:T(8,128)} copy(f32[8,5,128,128]{2,3,1,0:T(8,128)} %convolution_bitcast_fusion) | data formatting | bytes 5242880 | tf_op jit(solution)/shard_map/hnid,hnie->hnde/dot_general | solution.py:100
  117.9 5.7 %fusion.19 = f32[1,8,128,128]{3,0,2,1:T(1,128)} fusion(f32[8,5,128,128]{3,1,2,0:T(8,128)} %copy.42, f32[]{:T(128)} %bitcast.23, s32[5]{0:T(128)S(1)} %copy-done.15), kind=kOutput, calls=%fused_computation.40 | convolution fusion | flops 7864330 | bytes 3145752 | tf_op jit(solution)/shard_map/c,hcde->hde/dot_general | solution.py:107
  123.6 0.0 all-gather.8.cloned.1.call-update
  123.6 6.6 %fusion.13 = f32[8,128,128,5]{2,3,1,0:T(8,128)} fusion(f32[8,5,128,128]{3,1,2,0:T(8,128)} %copy.42, f32[5]{0:T(128)S(1)} %convert_element_type.51), kind=kOutput, calls=%fused_computation.35 | convolution fusion | flops 39321676 | bytes 5242900 | tf_op jit(solution)/shard_map/bc,hcde->hbde/dot_general | solution.py:103
  130.2 1.5 select_convert_fusion
  131.7 0.2 copy-done.7
  131.9 1.5 fusion.31
  133.4 0.0 copy-done.13
  133.5 2.4 %add_convert_fusion = bf16[8,5,256,128]{3,2,1,0:T(8,128)(2,1)} fusion(f32[8,5,256,128]{3,2,1,0:T(8,128)S(1)} %fusion.31, bf16[8,5,256,128]{3,2,1,0:T(8,128)(2,1)S(1)} %bitcast.114, bf16[8,5,128,128]{3,2,1,0:T(8,128)(2,1)S(1)} %copy-done.13), kind=kOutput, calls=%fused_computation.12 | convolution fusion | flops 338165760 | bytes 11796480 | tf_op jit(solution)/shard_map/hnie,hnde->hnid/dot_general | solution.py:120
  135.9 3.9 %fusion.33 = f32[8,5,256,128]{3,2,1,0:T(8,128)} fusion(bf16[8,5,256,256]{3,2,1,0:T(8,128)(2,1)S(1)} %bitcast.117, bf16[8,5,256,128]{3,2,1,0:T(8,128)(2,1)S(1)} %bitcast.115), kind=kOutput, calls=%fused_computation.58 | convolution fusion | flops 671088640 | bytes 13107200 | tf_op jit(solution)/shard_map/hnij,hnid->hnjd/dot_general | solution.py:97
  139.8 3.9 %fusion.32 = f32[8,5,256,128]{3,2,1,0:T(8,128)} fusion(bf16[8,5,256,256]{3,2,1,0:T(8,128)(2,1)S(1)} %select_convert_fusion, bf16[8,5,256,128]{3,2,1,0:T(8,128)(2,1)S(1)} %bitcast.110), kind=kOutput, calls=%fused_computation.57 | convolution fusion | flops 671088640 | bytes 13107200 | tf_op jit(solution)/shard_map/hnij,hnid->hnjd/dot_general | solution.py:94
  143.7 23.7 %all-gather.8.cloned.1.call-done = f32[32,128,128]{2,1,0:T(8,128)} async-done(((f32[8,128,128]{2,1,0:T(8,128)}), f32[32,128,128]{2,1,0:T(8,128)}) %all-gather.8.cloned.1.call-update) | async-done | bytes 2097168 | tf_op jit(solution)/shard_map/all_gather | solution.py:9
  167.5 13.6 %while.35 = (s32[]{:T(128)}, f32[]{:T(128)}, f32[8,128,128]{2,1,0:T(8,128)S(1)}, s32[]{:T(128)}, f32[4]{0:T(128)S(1)}, /*index=5*/f32[4,8,128,128]{3,2,1,0:T(8,1...) while((s32[]{:T(128)}, f32[]{:T(128)}, ...), condition=%wide.region_7.8_spmd.clone, body=%wide.region_6.7_spmd.clone.sunk | while | flops 524299 | bytes 1573110 | solution.py:22
  167.5 0.6 dynamic_slice.47
  169.3 1.5 fusion.63
  170.9 0.6 dynamic_slice.47
  172.7 1.5 fusion.63
  174.2 0.6 dynamic_slice.47
  176.1 1.5 fusion.63
  177.6 0.6 dynamic_slice.47
  179.5 1.5 fusion.63
  181.0 0.0 copy-start.8
  181.1 3.0 %fusion.8 = bf16[8,5,128,128]{3,2,1,0:T(8,128)(2,1)S(1)} fusion(f32[8,128,128,5]{2,3,1,0:T(8,128)} %fusion.13, f32[8,128,128]{2,1,0:T(8,128)S(1)} %get-tuple-element.271, f32[5]{0:T(128)S(1)} %compare_convert_fusion), kind=kLoop, calls=%fused_computation.22 | loop fusion | flops 1966080 | bytes 4456468 | tf_op jit(solution)/shard_map/convert_element_type | solution.py:119
  184.0 0.0 copy-done.8
  184.0 0.0 copy-start.11
  184.1 5.1 %fusion.2 = bf16[8,5,256,128]{3,2,1,0:T(8,128)(2,1)} fusion(f32[8,5,256,128]{3,2,1,0:T(8,128)} %fusion.33, bf16[8,5,256,128]{3,2,1,0:T(8,128)(2,1)S(1)} %bitcast.121, bf16[8,5,128,128]{3,2,1,0:T(8,128)(2,1)S(1)} %fusion.8), kind=kOutput, calls=%fused_computation.7 | convolution fusion | flops 338165760 | bytes 11796480 | tf_op jit(solution)/shard_map/hnid,hnde->hnie/dot_general | solution.py:126
  189.2 2.3 %fusion.3 = bf16[8,5,256,128]{3,2,1,0:T(8,128)(2,1)} fusion(f32[8,5,256,128]{3,2,1,0:T(8,128)S(1)} %bitcast.127, bf16[8,5,128,128]{3,2,1,0:T(8,128)(2,1)S(1)} %fusion.8, bf16[8,5,256,128]{3,2,1,0:T(8,128)(2,1)S(1)} %bitcast.125), kind=kOutput, calls=%fused_computation.9 | convolution fusion | flops 338165760 | bytes 11796480 | tf_op jit(solution)/shard_map/hnie,hnde->hnid/dot_general | solution.py:123
  (41 shorter events, 0.2 us)
Async XLA Ops:
  7.2 33.8 %copy-start = (bf16[8,1280,128]{2,1,0:T(8,128)(2,1)S(1)}, bf16[8,1280,128]{2,1,0:T(8,128)(2,1)}, u32[]{:S(2)}) copy-start(bf16[8,1280,128]{2,1,0:T(8,128)(2,1)} %param.10) | copy-start | bytes 7864324
  7.2 60.7 %all-gather.6.cloned.1.call-start = ((), (), s32[]{:S(2)}) async-start(), calls=%async_computation | async-start | bytes 2621440 | tf_op jit(solution)/shard_map/all_gather | solution.py:9
  9.3 4.9 %copy-start.15 = (s32[5]{0:T(128)S(1)}, s32[5]{0:T(128)}, u32[]{:S(2)}) copy-start(s32[5]{0:T(128)} %param.15) | copy-start | bytes 64
  12.7 1.5 copy-start.1
  19.0 148.4 %all-gather.8.cloned.1.call-start = ((), (), s32[]{:S(2)}) async-start(), calls=%async_computation.1 | async-start | bytes 2621440 | tf_op jit(solution)/shard_map/all_gather | solution.py:9
  33.6 7.4 %copy-start.6 = (bf16[8,1280,128]{2,1,0:T(8,128)(2,1)S(1)}, bf16[8,1280,128]{2,1,0:T(8,128)(2,1)}, u32[]{:S(2)}) copy-start(bf16[8,1280,128]{2,1,0:T(8,128)(2,1)} %param.11) | copy-start | bytes 7864324
  41.0 3.9 %copy-start.9 = (bf16[8,1280,128]{2,1,0:T(8,128)(2,1)S(1)}, bf16[8,1280,128]{2,1,0:T(8,128)(2,1)}, u32[]{:S(2)}) copy-start(bf16[8,1280,128]{2,1,0:T(8,128)(2,1)} %param.12) | copy-start | bytes 7864324
  42.5 2.3 %copy-start.4 = (bf16[8,5,256,256]{3,2,1,0:T(8,128)(2,1)}, bf16[8,5,256,256]{3,2,1,0:T(8,128)(2,1)S(1)}, u32[]{:S(2)}) copy-start(bf16[8,5,256,256]{3,2,1,0:T(8,128)(2,1)S(1)} %select_convert_fusion.1) | copy-start | bytes 15728644
  81.4 3.7 %copy-start.5 = (f32[8,5,256,128]{3,2,1,0:T(8,128)S(1)}, f32[8,5,256,128]{3,2,1,0:T(8,128)}, u32[]{:S(2)}) copy-start(f32[8,5,256,128]{3,2,1,0:T(8,128)} %fusion.29) | copy-start | bytes 15728644
  85.2 3.2 %copy-start.12 = (bf16[8,5,128,128]{3,2,1,0:T(8,128)(2,1)}, bf16[8,5,128,128]{3,2,1,0:T(8,128)(2,1)S(1)}, u32[]{:S(2)}) copy-start(bf16[8,5,128,128]{3,2,1,0:T(8,128)(2,1)S(1)} %fusion.9) | copy-start | bytes 3932164
  85.2 8.5 %copy-start.14 = (f32[8,128]{1,0:T(8,128)S(1)}, f32[8,128]{1,0:T(8,128)}, u32[]{:S(2)}) copy-start(f32[8,128]{1,0:T(8,128)} %param.14) | copy-start | bytes 12292
  109.2 1.5 copy-start.2
  123.6 6.6 %copy-start.3 = (bf16[8,1280,128]{2,1,0:T(8,128)(2,1)S(1)}, bf16[8,1280,128]{2,1,0:T(8,128)(2,1)}, u32[]{:S(2)}) copy-start(bf16[8,1280,128]{2,1,0:T(8,128)(2,1)} %copy-done.2) | copy-start | bytes 7864324
  123.6 6.6 %copy-start.10 = (bf16[8,1280,128]{2,1,0:T(8,128)(2,1)S(1)}, bf16[8,1280,128]{2,1,0:T(8,128)(2,1)}, u32[]{:S(2)}) copy-start(bf16[8,1280,128]{2,1,0:T(8,128)(2,1)} %param.12) | copy-start | bytes 7864324
  130.2 1.7 copy-start.7
  130.2 5.7 %slice-start = ((s8[5242880]{0:T(1024)(128)(4,1)}), s8[4194304]{0:T(1024)(128)(4,1)S(1)}, s32[]{:S(2)}) async-start(s8[5242880]{0:T(1024)(128)(4,1)} %bitcast.116), calls=%async_computation.2 | async-start | bytes 8388608
  131.9 1.6 copy-start.13
  131.9 4.0 %slice-start.1 = ((s8[5242880]{0:T(1024)(128)(4,1)}), s8[1048576]{0:T(1024)(128)(4,1)S(1)}, s32[]{:S(2)}) async-start(s8[5242880]{0:T(1024)(128)(4,1)} %bitcast.116), calls=%async_computation.3 | async-start | bytes 2097152
  181.0 3.0 %copy-start.8 = (bf16[8,1280,128]{2,1,0:T(8,128)(2,1)S(1)}, bf16[8,1280,128]{2,1,0:T(8,128)(2,1)}, u32[]{:S(2)}) copy-start(bf16[8,1280,128]{2,1,0:T(8,128)(2,1)} %param.11) | copy-start | bytes 7864324
  181.1 8.1 %slice-start.2 = ((s8[5242880]{0:T(1024)(128)(4,1)}), s8[4194304]{0:T(1024)(128)(4,1)S(1)}, s32[]{:S(2)}) async-start(s8[5242880]{0:T(1024)(128)(4,1)} %bitcast.126), calls=%async_computation.4 | async-start | bytes 8388608
  184.0 5.1 %copy-start.11 = (bf16[8,1280,128]{2,1,0:T(8,128)(2,1)S(1)}, bf16[8,1280,128]{2,1,0:T(8,128)(2,1)}, u32[]{:S(2)}) copy-start(bf16[8,1280,128]{2,1,0:T(8,128)(2,1)} %param.12) | copy-start | bytes 7864324
  184.1 5.1 %slice-start.3 = ((s8[5242880]{0:T(1024)(128)(4,1)}), s8[1048576]{0:T(1024)(128)(4,1)S(1)}, s32[]{:S(2)}) async-start(s8[5242880]{0:T(1024)(128)(4,1)} %bitcast.126), calls=%async_computation.5 | async-start | bytes 2097152
Sparse Core Ops, SparseCore 0:
  19.2 48.6 all-gather.5
  123.7 43.7 all-gather.7
